TPU v7x, 128 devices: a whole 4x4x4 slice. The times are simulated.
128 devices in a mesh: child: 2 (over z_hi), row: 8 (over y, core), col: 8 (over x, z_lo).
Axes of the slice: x: 4, y: 4, z: 4 (z_hi: 2, z_lo: 2; z = z_hi * 2 + z_lo), core: 2. Of those that a mesh axis runs over, the one named last changes fastest.
Arguments:
- child_fronts: float32 [2, 8192, 8192], P('child', 'row', 'col')
- parent_front: float32 [12288, 12288], P('row', ('child', 'col')), may hold values from -6 to 6
- index_maps: int32 [2, 8192], replicated, may hold values from 0 to 12287, as said below
- orders: int32 [2], replicated, may hold values from 4096 to 8192, as said below
Outputs:
- assembled: float32 [12288, 12288], P('row', ('child', 'col'))
- panel_factor: float32 [2, 8192, 512], P('child', 'row')
Inputs may be any that keep to these rules, and one draw needn't show every extreme that they name: For each child, index_maps is one to one. Cut the child indices into aligned blocks of 8192 / 8 and the parent indices into 2 * 8 aligned slices of 12288 / (2 * 8): each block sends exactly 8192 / (2 * 8 * 8) of its indices into each slice. `orders`: one child's order is 8192.
All inputs are finite; a program needn't handle non-finite values.
Results may differ from a plain program's by a relative error of at most 0.0001.
Values sent between devices are 32-bit elements; how exact they have to be, the bound alone decides.
No kernel may reach another device: no remote copies, remote signals or barrier semaphores. Data moves between devices by JAX's collectives and lax.ppermute only.
A program may use at most 128 MiB of HBM per device.

v0:
```python
import jax
import jax.numpy as jnp
from jax import lax
from jax.sharding import PartitionSpec as P

PANEL = 512
FRONT = 8192


def from_root(value, axis, source):
    kept = jnp.where(lax.axis_index(axis) == source, value, 0).astype(value.dtype)
    return lax.psum(kept, axis)


def select_rows(parent_map, owner, width, count):
    everywhere = jnp.arange(FRONT, dtype=jnp.int32)
    keyed = jnp.where(parent_map // width == owner, everywhere, everywhere + FRONT)
    chosen = jnp.argsort(keyed)[:count]
    return parent_map[chosen] - owner * width


def invert_slots(slots, length):
    count = slots.shape[0]
    lookup = jnp.full((length,), count, jnp.int32)
    return lookup.at[slots].set(jnp.arange(count, dtype=jnp.int32))


def factor_panel(corner, columns, global_rows, own_order):
    diag_factor = jnp.linalg.cholesky(corner)
    solved = lax.linalg.triangular_solve(
        diag_factor, columns, left_side=False, lower=True, transpose_a=True
    )
    top_rows = jnp.pad(diag_factor, ((0, columns.shape[0] - PANEL), (0, 0)))
    result = jnp.where(global_rows[:, None] < PANEL, top_rows, solved)
    return jnp.where(global_rows[:, None] < own_order, result, jnp.float32(0.0))


def on_device(child_fronts, parent_front, index_maps, orders):
    block_here = child_fronts[0]
    rows_here, cols_here = block_here.shape
    child_index = lax.axis_index("child")
    row_index = lax.axis_index("row")
    col_index = lax.axis_index("col")
    n_row = lax.axis_size("row")
    n_col = lax.axis_size("col")
    own_map = lax.dynamic_index_in_dim(index_maps, child_index, 0, keepdims=False)
    own_order = lax.dynamic_index_in_dim(orders, child_index, 0, keepdims=False)
    global_rows = row_index * rows_here + jnp.arange(rows_here, dtype=jnp.int32)
    global_cols = col_index * cols_here + jnp.arange(cols_here, dtype=jnp.int32)
    corner = from_root(block_here[:PANEL, :PANEL], ("row", "col"), 0)
    columns = from_root(block_here[:, :PANEL], "col", 0)
    own_panel = factor_panel(corner, columns, global_rows, own_order)
    other_panel = from_root(own_panel, "row", col_index)
    update = block_here - jnp.dot(own_panel, other_panel.T, precision=lax.Precision.HIGHEST)
    live_rows = (global_rows >= PANEL) & (global_rows < own_order)
    live_cols = (global_cols >= PANEL) & (global_cols < own_order)
    update = jnp.where(live_rows[:, None] & live_cols[None, :], update, jnp.float32(0.0))
    parent_rows, parent_cols = parent_front.shape
    row_map = lax.dynamic_slice_in_dim(own_map, row_index * rows_here, rows_here)
    col_map = lax.dynamic_slice_in_dim(own_map, col_index * cols_here, cols_here)
    row_keys = row_map // parent_rows * rows_here + jnp.arange(rows_here, dtype=jnp.int32)
    col_keys = col_map // parent_cols * cols_here + jnp.arange(cols_here, dtype=jnp.int32)
    sorted_block = update[jnp.argsort(row_keys)][:, jnp.argsort(col_keys)]
    part_rows = rows_here // n_row
    part_cols = cols_here // (2 * n_col)
    pieces = (
        sorted_block.reshape(n_row, part_rows, 2, n_col, part_cols)
        .transpose(2, 0, 3, 1, 4)
        .reshape(-1, part_cols)
    )
    arrived = lax.all_to_all(
        pieces, ("child", "row", "col"), split_axis=0, concat_axis=0, tiled=True
    )
    arrived = (
        arrived.reshape(2, n_row, n_col, part_rows, part_cols)
        .transpose(0, 1, 3, 2, 4)
        .reshape(2, rows_here, n_col * part_cols)
    )
    col_owner = child_index * n_col + col_index
    assembled = parent_front
    for source in range(2):
        parent_map = index_maps[source]
        row_slots = select_rows(parent_map, row_index, parent_rows, rows_here)
        col_slots = select_rows(parent_map, col_owner, parent_cols, n_col * part_cols)
        row_lookup = invert_slots(row_slots, parent_rows)
        col_lookup = invert_slots(col_slots, parent_cols)
        padded = jnp.pad(arrived[source], ((0, 1), (0, 1)))
        placed = jnp.take(jnp.take(padded, row_lookup, axis=0), col_lookup, axis=1)
        assembled = assembled + placed
    return (assembled, own_panel[None])


def solution(mesh):
    in_specs = (P("child", "row", "col"), P("row", ("child", "col")), P(), P())
    out_specs = (P("row", ("child", "col")), P("child", "row", None))
    return jax.shard_map(
        on_device, mesh=mesh, in_specs=in_specs, out_specs=out_specs, check_vma=False
    )
```

profile of v0, /device:TPU:0, one launch (start us, length us, event | category | flops | bytes accessed | tf_op | source)
XLA Modules:
  0.0 977.2 jit_solution(15241625877835123751)
XLA Ops:
  20.0 6.8 sort.95
  27.3 6.8 sort.93
  34.7 533.7 %all-reduce.8.cloned.1.call-done = f32[512,512]{0,1:T(8,128)} async-done(((f32[512,512]{0,1:T(8,128)}), f32[512,512]{0,1:T(8,128)}) %all-reduce.8.cloned.1.call-update) | async-done | bytes 1048592 | tf_op jit(solution)/shard_map/psum | solution.py:12
  571.4 11.7 %cholesky.103 = f32[128,128]{1,0:T(8,128)S(1)} custom-call(f32[128,128]{1,0:T(8,128)S(1)} %cholesky.263), custom_call_target="Cholesky" | custom-call | tf_op jit(solution)/shard_map/jit(cholesky)/cholesky | solution.py:29
  583.2 10.2 %custom-call.30 = f32[1,128,128]{1,2,0:T(8,128)S(1)} custom-call(f32[1,128,128]{2,1,0:T(8,128)S(1)} %get-tuple-element.63), custom_call_target="InvertDiagBlocksLowerTriangular" | custom-call | tf_op jit(solution)/shard_map/jit(cholesky)/cholesky | solution.py:29
  594.3 11.7 %cholesky.215 = f32[128,128]{1,0:T(8,128)S(1)} custom-call(f32[128,128]{1,0:T(8,128)S(1)} %cholesky.267), custom_call_target="Cholesky" | custom-call | tf_op jit(solution)/shard_map/jit(cholesky)/cholesky | solution.py:29
  606.1 9.8 %custom-call.31 = f32[1,128,128]{1,2,0:T(8,128)S(1)} custom-call(f32[1,128,128]{2,1,0:T(8,128)S(1)} %get-tuple-element.61), custom_call_target="InvertDiagBlocksLowerTriangular" | custom-call | tf_op jit(solution)/shard_map/jit(cholesky)/cholesky | solution.py:29
  617.0 11.9 %cholesky.236 = f32[128,128]{1,0:T(8,128)S(1)} custom-call(f32[128,128]{1,0:T(8,128)S(1)} %cholesky.272), custom_call_target="Cholesky" | custom-call | tf_op jit(solution)/shard_map/jit(cholesky)/cholesky | solution.py:29
  629.0 9.8 %custom-call.32 = f32[1,128,128]{1,2,0:T(8,128)S(1)} custom-call(f32[1,128,128]{2,1,0:T(8,128)S(1)} %get-tuple-element.59), custom_call_target="InvertDiagBlocksLowerTriangular" | custom-call | tf_op jit(solution)/shard_map/jit(cholesky)/cholesky | solution.py:29
  639.6 11.7 %cholesky.253 = f32[128,128]{1,0:T(8,128)S(1)} custom-call(f32[128,128]{1,0:T(8,128)S(1)} %convolution_subtract_fusion.4), custom_call_target="Cholesky" | custom-call | tf_op jit(solution)/shard_map/jit(cholesky)/cholesky | solution.py:29
  656.3 11.0 %while.1 = (s32[]{:T(128)}, f32[512,512]{0,1:T(8,128)S(1)}, s32[4,2]{0,1:T(2,128)S(1)}, f32[4,128,128]{2,1,0:T(8,128)}, s32[]{:T(128)}) while((s32[]{:T(128)}, f32[512,512]{0,1:T(8,128)S(1)}, s32[4,2]{0,1:T(2,128)S(1)}, f32[4,128,128]{2,1,0:T(8,128)}, s32[]{:T(128)}) %tuple.45), condition=%wide.while_cond, body=%wide.while_body.sunk | while | flops 2 | bytes 393329 | solution.py:30
  667.3 40.6 %custom-call.33 = f32[4,128,128]{1,2,0:T(8,128)S(1)} custom-call(f32[4,128,128]{2,1,0:T(8,128)} %get-tuple-element.23), custom_call_target="InvertDiagBlocksLowerTriangular" | custom-call | tf_op jit(solution)/shard_map/triangular_solve | solution.py:30
  728.1 6.8 sort.94
  734.9 6.9 sort.92
  742.5 40.9 %all-reduce.12.cloned.1.call-done = f32[1024,512]{0,1:T(8,128)} async-done(((f32[1024,512]{0,1:T(8,128)}), f32[1024,512]{0,1:T(8,128)}) %all-reduce.12.cloned.1.call-update) | async-done | bytes 2097168 | tf_op jit(solution)/shard_map/psum | solution.py:12
  783.4 10.7 %subtract_select_fusion = f32[1024,1024]{0,1:T(8,128)} fusion(f32[1024,512]{0,1:T(8,128)} %all-reduce.12.cloned.1.call-done, pred[1024]{0:T(1024)(128)(4,1)S(1)} %fusion.60, pred[1024]{0:T(1024)(128)(4,1)S(1)} %fusion.61, f32[1,1024,1024]{1,2,0:T(8,128)} %copy.24, f32[1024,128]{0,1:T(8,128)S(1)} %fusion.25, f32[1024,128]{0,1:T(8,128)S(1)} %fusion.26, ...), kind=kOutput, calls=%fused_computation.18 | convolution fusion | flops 6448218112 | bytes 13635584 | tf_op jit(solution)/shard_map/dot_general | solution.py:54
  799.5 8.5 gather_fusion
  813.3 8.5 gather_fusion.1
  827.8 8.7 all-to-all-start
  855.3 6.2 copy.41
  877.4 11.2 %all-to-all-done = f32[128,128,64]{1,2,0:T(8,128)} async-done(((f32[128,128,64]{1,2,0:T(8,128)}), f32[128,128,64]{1,2,0:T(8,128)}, u32[]{:S(2)}, u32[]{:S(2)}) %all-to-all-start) | async-done | bytes 4194336 | tf_op jit(solution)/shard_map/all_to_all | solution.py:71
  926.8 7.9 gather_fusion.8
  948.3 8.0 gather_fusion.9
  956.3 8.0 bitcast_add_fusion
  (160 shorter events, 162.9 us)
Async XLA Ops:
  7.2 561.2 %all-reduce.8.cloned.1.call-start = ((), (), s32[]{:S(2)}) async-start(), calls=%async_computation.1 | async-start | bytes 2097152 | tf_op jit(solution)/shard_map/psum | solution.py:12
  14.9 3.4 copy-start.3
  14.9 3.7 copy-start.6
  14.9 693.0 %all-reduce.10.cloned.1.call-start = ((), (), s32[]{:S(2)}) async-start(), calls=%async_computation.2 | async-start | bytes 4194304 | tf_op jit(solution)/shard_map/psum | solution.py:12
  18.2 765.3 %all-reduce.12.cloned.1.call-start = ((), (), s32[]{:S(2)}) async-start(), calls=%async_computation.3 | async-start | bytes 4194304 | tf_op jit(solution)/shard_map/psum | solution.py:12
  667.3 44.7 %copy-start.1 = (f32[512,512]{0,1:T(8,128)}, f32[512,512]{0,1:T(8,128)S(1)}, u32[]{:S(2)}) copy-start(f32[512,512]{0,1:T(8,128)S(1)} %get-tuple-element.132) | copy-start | bytes 3145732
  707.9 4.1 copy-start.2
  827.8 8.7 copy-start.5
  827.8 60.7 %all-to-all-start = ((f32[128,128,64]{1,2,0:T(8,128)}), f32[128,128,64]{1,2,0:T(8,128)}, u32[]{:S(2)}, u32[]{:S(2)}) async-start(f32[128,128,64]{1,2,0:T(8,128)} %bitcast.99), calls=%async_computation | async-start | bytes 8388608 | tf_op jit(solution)/shard_map/all_to_all | solution.py:71
  839.7 12.3 %copy-start.4 = (s32[512]{0:T(512)S(1)}, s32[512]{0:T(512)}, u32[]{:S(2)}) copy-start(s32[512]{0:T(512)} %compare_select_fusion.13) | copy-start | bytes 6148
  855.3 20.1 %copy-start = (f32[1,1024,512]{1,2,0:T(8,128)S(1)}, f32[1,1024,512]{1,2,0:T(8,128)}, u32[]{:S(2)}) copy-start(f32[1,1024,512]{1,2,0:T(8,128)} %get-tuple-element.52) | copy-start | bytes 6291460
Sparse Core Ops, SparseCore 0:
  15.0 553.3 all-reduce.7
  571.6 104.0 all-reduce.9
  718.8 64.5 all-reduce.11
where the time goes:
time: 988 us; the launch traced here: 977 us
  waiting for transfers between devices  586 us (59%)
  other arithmetic  185 us (19%)
  local copies, waits for them, and re-layouts  158 us (16%)
  matrix products  21.1 us (2%)
  between operations  17.4 us (2%)
    psum x3, waiting for transfers between devices, from_root(): return lax.psum(kept, axis)  575 us
    another operation x14, other arithmetic, factor_panel(): diag_factor = jnp.linalg.cholesky(corner)  79 us
    another operation x3, other arithmetic, factor_panel(): lax.linalg.triangular_solve(diag_factor, columns, left_side=False, lower=...  40.8 us
    sort x4, other arithmetic, select_rows(): chosen = jnp.argsort(keyed)[:count]  27.2 us
    gather x4, local copies, waits for them, and re-layouts, on_device(): placed = jnp.take(jnp.take(padded, row_lookup, axis=0), col_lookup, axis=1)  25.4 us
    unnamed x19, local copies, waits for them, and re-layouts  22.8 us
    gather x3, local copies, waits for them, and re-layouts, on_device(): sorted_block = update[jnp.argsort(row_keys)][:, jnp.argsort(col_keys)]  22.4 us
  transfers between devices with their start and end apart: 4, of which 3 were waited for; matrix products, arithmetic and copies ran while one was open for 23% of the time, Pallas kernels for 0%

commit v1 on v0

--- a/solution.py
+++ b/solution.py
@@ -9,7 +9,7 @@
 
 def from_root(value, axis, source):
     kept = jnp.where(lax.axis_index(axis) == source, value, 0).astype(value.dtype)
-    return lax.psum(kept, axis)
+    return jnp.sum(lax.all_gather(kept, axis), axis=0)
 
 
 def select_rows(parent_map, owner, width, count):

time: 988 us -> 1180 us (1.19)
  waiting for transfers between devices: 586 us -> 748 us
  other arithmetic: 185 us -> 223 us
    all_gather x0 -> x3, waiting for transfers between devices: none -> 735 us  [from_root(): return jnp.sum(lax.all_gather(kept, axis), axis=0)]
    psum x3 -> x0, waiting for transfers between devices: 575 us -> none  [from_root(): return lax.psum(kept, axis)]
    reduce_sum x0 -> x3, other arithmetic: none -> 40.2 us  [from_root(): return jnp.sum(lax.all_gather(kept, axis), axis=0)]
  transfers between devices with their start and end apart: 4 -> 4, of which waited for: 3 -> 4; matrix products, arithmetic and copies ran while one was open for 23% -> 8% of each run, Pallas kernels for 0% -> 0%
where the time goes in v1:
time: 1180 us
  waiting for transfers between devices  748 us (63%)
  other arithmetic  223 us (19%)
  local copies, waits for them, and re-layouts  147 us (12%)
  matrix products  31 us (3%)
  between operations  17.2 us (1%)
    all_gather x3, waiting for transfers between devices, from_root(): return jnp.sum(lax.all_gather(kept, axis), axis=0)  735 us
    another operation x14, other arithmetic, factor_panel(): diag_factor = jnp.linalg.cholesky(corner)  78.6 us
    another operation x3, other arithmetic, factor_panel(): lax.linalg.triangular_solve(diag_factor, columns, left_side=False, lower=...  40.7 us
    reduce_sum x3, other arithmetic, from_root(): return jnp.sum(lax.all_gather(kept, axis), axis=0)  40.2 us
    sort x4, other arithmetic, select_rows(): chosen = jnp.argsort(keyed)[:count]  27.2 us
    gather x4, local copies, waits for them, and re-layouts, on_device(): placed = jnp.take(jnp.take(padded, row_lookup, axis=0), col_lookup, axis=1)  25.4 us
  transfers between devices with their start and end apart: 4, of which 4 were waited for; matrix products, arithmetic and copies ran while one was open for 8% of the time, Pallas kernels for 0%

profile of v1, /device:TPU:0, one launch (start us, length us, event | category | flops | bytes accessed | tf_op | source)
XLA Modules:
  0.0 1178.0 jit_solution(11134578235207406597)
XLA Ops:
  14.2 324.6 %all-gather.9.cloned.1.call-done = f32[8192,512]{1,0:T(8,128)} async-done(((f32[1024,512]{1,0:T(8,128)}), f32[8192,512]{1,0:T(8,128)}) %all-gather.9.cloned.1.call-update) | async-done | bytes 16777232 | tf_op jit(solution)/shard_map/all_gather | solution.py:12
  338.7 9.4 reduce_sum.28
  348.1 361.7 %all-gather.7.cloned.1.call-done = f32[32768,512]{1,0:T(8,128)} async-done(((f32[512,512]{1,0:T(8,128)}), f32[32768,512]{1,0:T(8,128)}) %all-gather.7.cloned.1.call-update) | async-done | bytes 67108880 | tf_op jit(solution)/shard_map/all_gather | solution.py:12
  709.9 21.4 %reduce_sum.27 = f32[512,512]{1,0:T(8,128)S(1)} reduce(f32[64,512,512]{2,1,0:T(8,128)} %bitcast.7, f32[]{:T(128)} %constant.247.clone.1), dimensions={0}, to_apply=%region_0.1 | reduce | flops 16515072 | bytes 68157440 | tf_op jit(solution)/shard_map/reduce_sum | solution.py:12
  732.8 11.7 cholesky.103
  744.7 9.8 custom-call.30
  757.0 11.7 cholesky.215
  768.8 10.0 custom-call.31
  780.3 11.7 cholesky.236
  792.8 9.8 custom-call.32
  804.0 11.7 cholesky.253
  821.0 11.7 while.1
  832.7 39.3 %custom-call.33 = f32[4,128,128]{1,2,0:T(8,128)S(1)} custom-call(f32[4,128,128]{2,1,0:T(8,128)S(1)} %get-tuple-element.23), custom_call_target="InvertDiagBlocksLowerTriangular" | custom-call | tf_op jit(solution)/shard_map/triangular_solve | solution.py:30
  920.1 6.9 sort.95
  928.5 48.2 %all-gather.11.cloned.1.call-done = f32[8192,512]{1,0:T(8,128)} async-done(((f32[1024,512]{1,0:T(8,128)}), f32[8192,512]{1,0:T(8,128)}) %all-gather.11.cloned.1.call-update) | async-done | bytes 16777232 | tf_op jit(solution)/shard_map/all_gather | solution.py:12
  976.7 9.4 reduce_sum.29
  986.2 11.4 subtract_select_fusion
  997.6 8.6 gather_fusion
  1011.5 8.6 gather_fusion.1
  1026.1 11.3 all-to-all-start
  1076.2 13.2 %all-to-all-done = f32[128,128,64]{1,2,0:T(8,128)} async-done(((f32[128,128,64]{1,2,0:T(8,128)}), f32[128,128,64]{1,2,0:T(8,128)}, u32[]{:S(2)}, u32[]{:S(2)}) %all-to-all-start) | async-done | bytes 4194336 | tf_op jit(solution)/shard_map/all_to_all | solution.py:71
  1127.7 7.9 gather_fusion.8
  1149.2 8.0 gather_fusion.9
  1157.1 8.0 bitcast_add_fusion
  (140 shorter events, 186.4 us)
Async XLA Ops:
  7.2 331.6 %all-gather.9.cloned.1.call-start = ((), (), s32[]{:S(2)}) async-start(), calls=%async_computation.2 | async-start | bytes 18874368 | tf_op jit(solution)/shard_map/all_gather | solution.py:12
  7.2 5.6 copy-start.3
  10.4 699.5 %all-gather.7.cloned.1.call-start = ((), (), s32[]{:S(2)}) async-start(), calls=%async_computation.1 | async-start | bytes 68157440 | tf_op jit(solution)/shard_map/all_gather | solution.py:12
  12.8 964.0 %all-gather.11.cloned.1.call-start = ((), (), s32[]{:S(2)}) async-start(), calls=%async_computation.3 | async-start | bytes 18874368 | tf_op jit(solution)/shard_map/all_gather | solution.py:12
  731.8 1.0 copy-start.1
  886.8 0.8 copy-start
  887.6 3.0 copy-start.2
  1026.1 63.3 %all-to-all-start = ((f32[128,128,64]{1,2,0:T(8,128)}), f32[128,128,64]{1,2,0:T(8,128)}, u32[]{:S(2)}, u32[]{:S(2)}) async-start(f32[128,128,64]{1,2,0:T(8,128)} %bitcast.100), calls=%async_computation | async-start | bytes 8388608 | tf_op jit(solution)/shard_map/all_to_all | solution.py:71
Sparse Core Ops, SparseCore 0:
  10.5 328.1 all-gather.8
  341.0 368.8 all-gather.6
  890.7 85.9 all-gather.10
